TPU v7x, 512 devices: a whole 4x4x16 slice. The times are simulated.
512 devices in a mesh: head: 8 (over x, core), expert: 64 (over z, y).
Axes of the slice: x: 4, y: 4, z: 16, core: 2. Of those that a mesh axis runs over, the one named last changes fastest.
Arguments:
- q_latent: bfloat16 [512, 64, 512], P('expert', 'head'), may hold values from -16 to 16
- q_rotary: bfloat16 [512, 64, 64], P('expert', 'head'), may hold values from -3 to 3
- cache_latent: bfloat16 [512, 128, 512], P('expert'), may hold values from -5 to 5
- cache_rotary: bfloat16 [512, 64, 128], P('expert'), may hold values from -5 to 5
- lengths: int32 [512], P('expert'), may hold values from 16 to 128, as said below
- w_value_out: bfloat16 [32768, 5120], P('head', 'expert'), may hold values from -0.25 to 0.25
- resid: bfloat16 [512, 5120], P('expert'), may hold values from -8 to 8
- norm_gain: float32 [5120], replicated, may hold values from 0.1 to 1.9
- route_ids: int32 [512, 6], P('expert'), may hold values from 0 to 63, as said below
- route_weights: float32 [512, 6], P('expert'), may hold values from 0.1 to 0.6
- w_gate_up: bfloat16 [64, 2, 768, 5120], P('expert', None, 'head'), may hold values from -0.078125 to 0.078125
- w_down: bfloat16 [64, 768, 5120], P('expert', 'head'), may hold values from -0.21875 to 0.21875
Outputs:
- mixed_out: float32 [512, 5120], P('expert', 'head')
Inputs may be any that keep to these rules, and one draw needn't show every extreme that they name: `lengths`: slots at positions below a sequence's length are valid; some sequence has length 128. `route_ids`: each row names 6 different experts. Among the rows of one device (aligned blocks of 8 rows) no expert is named by more than 2 rows, and one expert is named by exactly 2 rows in every block.
All inputs are finite; a program needn't handle non-finite values.
Results may differ from a plain program's by a relative error of at most 0.0046.
Values may be sent and summed in bfloat16 or wider, within the bound.
No kernel may reach another device: no remote copies, remote signals or barrier semaphores. Data moves between devices by JAX's collectives and lax.ppermute only.
A program may use at most 64 MiB of HBM per device.

v0:
```python
import jax
import jax.numpy as jnp
from jax import lax
from jax.sharding import PartitionSpec as P

softmax_scale = 192.0 ** (-0.5)
norm_epsilon = 1e-06


def attend(q_latent, q_rotary, cache_latent, cache_rotary, lengths):
    scores = jnp.einsum("shl,scl->shc", q_latent, cache_latent, preferred_element_type=jnp.float32)
    scores = scores + jnp.einsum(
        "shr,src->shc", q_rotary, cache_rotary, preferred_element_type=jnp.float32
    )
    scores = scores * softmax_scale
    position = lax.broadcasted_iota(jnp.int32, scores.shape, 2)
    scores = jnp.where(position < lengths[:, None, None], scores, -1e30)
    highest = jnp.max(scores, axis=2, keepdims=True)
    weights = jnp.exp(scores - highest)
    probs = (weights / jnp.sum(weights, axis=2, keepdims=True)).astype(jnp.bfloat16)
    return jnp.einsum(
        "shc,scl->shl", probs, cache_latent, preferred_element_type=jnp.float32
    ).astype(jnp.bfloat16)


def on_device(
    q_latent,
    q_rotary,
    cache_latent,
    cache_rotary,
    lengths,
    w_value_out,
    resid,
    norm_gain,
    route_ids,
    route_weights,
    w_gate_up,
    w_down,
):
    seq_local = q_latent.shape[0]
    latent_out = attend(q_latent, q_rotary, cache_latent, cache_rotary, lengths)
    flattened = latent_out.reshape(seq_local, -1)
    column_terms = jnp.dot(
        lax.all_gather(flattened, "expert", axis=0, tiled=True),
        w_value_out,
        preferred_element_type=jnp.float32,
    )
    column_sums = lax.psum(column_terms, "head")
    attention = lax.all_to_all(
        column_sums.astype(jnp.bfloat16), "expert", split_axis=0, concat_axis=1, tiled=True
    )
    stream = resid.astype(jnp.float32) + attention.astype(jnp.float32)
    mean_square = jnp.mean(stream * stream, axis=1, keepdims=True)
    normed = (stream * lax.rsqrt(mean_square + norm_epsilon) * norm_gain).astype(jnp.bfloat16)
    expert_count = lax.axis_size("expert")
    top_count = route_ids.shape[1]
    capacity = max(2, -(-(seq_local * top_count) // expert_count))
    flat_ids = route_ids.reshape(-1)
    one_hot = (flat_ids[:, None] == jnp.arange(expert_count, dtype=jnp.int32)[None, :]).astype(
        jnp.int32
    )
    earlier = jnp.cumsum(one_hot, axis=0) - one_hot
    slot_index = jnp.sum(earlier * one_hot, axis=1)
    target = (flat_ids * capacity + slot_index).reshape(seq_local, top_count)
    places = jnp.arange(expert_count * capacity, dtype=jnp.int32)
    matches = target[None, :, :] == places[:, None, None]
    selector = jnp.sum(matches.astype(jnp.int32), axis=2).astype(jnp.bfloat16)
    blending = jnp.sum(jnp.where(matches, route_weights[None, :, :], 0.0), axis=2)
    gate_up = w_gate_up[0]
    down_local = w_down[0]
    col_width = stream.shape[1] // lax.axis_size("head")
    offset = lax.axis_index("head") * col_width
    normed_cols = lax.dynamic_slice_in_dim(normed, offset, col_width, 1)
    outgoing = jnp.dot(selector, normed_cols, preferred_element_type=jnp.float32).astype(
        jnp.bfloat16
    )
    outgoing = outgoing.reshape(expert_count, capacity, -1)
    arrived = lax.all_to_all(outgoing, "expert", split_axis=0, concat_axis=0, tiled=True)
    arrived_cols = arrived.reshape(-1, arrived.shape[2])
    flat_rows = lax.all_gather(arrived_cols, "head", axis=1, tiled=True)
    projected = jnp.einsum("rd,gfd->rgf", flat_rows, gate_up, preferred_element_type=jnp.float32)
    hidden = (jax.nn.silu(projected[:, 0]) * projected[:, 1]).astype(jnp.bfloat16)
    partial_rows = jnp.dot(hidden, down_local, preferred_element_type=jnp.float32)
    summed_cols = lax.psum_scatter(
        partial_rows.astype(jnp.bfloat16), "head", scatter_dimension=1, tiled=True
    )
    summed_rows = summed_cols.reshape(expert_count, capacity, -1)
    returned = lax.all_to_all(summed_rows, "expert", split_axis=0, concat_axis=0, tiled=True)
    back_rows = returned.reshape(expert_count * capacity, -1).astype(jnp.float32)
    mixture = jnp.dot(blending.T, back_rows, precision=lax.Precision.HIGHEST)
    stream_cols = lax.dynamic_slice_in_dim(stream, offset, col_width, 1)
    return stream_cols + mixture


def solution(mesh):
    placed = (
        P("expert", "head", None),
        P("expert", "head", None),
        P("expert", None, None),
        P("expert", None, None),
        P("expert"),
        P("head", "expert"),
        P("expert", None),
        P(),
        P("expert", None),
        P("expert", None),
        P("expert", None, "head", None),
        P("expert", "head", None),
    )
    return jax.shard_map(
        on_device, mesh=mesh, in_specs=placed, out_specs=P("expert", "head"), check_vma=False
    )
```

profile of v0, /device:TPU:7, one launch (start us, length us, event | category | flops | bytes accessed | tf_op | source)
XLA Modules:
  0.0 349.5 jit_solution(5322238232163485525)
XLA Ops:
  6.5 1.8 fusion.21
  8.3 1.1 fusion.8
  9.4 0.2 fusion.20
  9.6 1.5 fusion.4
  11.1 0.7 copy.24
  11.8 0.1 eq.28
  12.0 0.2 select_reduce_fusion.1
  12.3 142.5 %all-gather.3.cloned.1.call-done = bf16[512,4096]{1,0:T(8,128)(2,1)} async-done(((bf16[8,4096]{1,0:T(8,128)(2,1)}), bf16[512,4096]{1,0:T(8,128)(2,1)}) %all-gather.3.cloned.1.call-update) | async-done | bytes 4194320 | tf_op jit(solution)/shard_map/all_gather | solution.py:44
  154.8 3.6 %fusion.22 = f32[512,80]{0,1:T(8,128)S(1)} fusion(bf16[512,4096]{1,0:T(8,128)(2,1)} %all-gather.3.cloned.1.call-done, bf16[4096,80]{0,1:T(8,128)(2,1)S(1)} %copy-done.1), kind=kOutput, calls=%fused_computation.40 | convolution fusion | flops 335544320 | bytes 5013504 | tf_op jit(solution)/shard_map/dot_general | solution.py:43
  158.4 31.2 %all-reduce.1 = bf16[512,80]{0,1:T(8,128)(2,1)S(1)} all-reduce(f32[512,80]{0,1:T(8,128)S(1)} %fusion.22), channel_id=1, replica_groups=mesh['head'=8,'expert'=64] {'head'}, use_global_device_ids=true, to_apply=%region_2.3 | all-reduce | flops 40960 | bytes 245760 | tf_op jit(solution)/shard_map/psum | solution.py:48
  189.6 0.7 copy.18
  190.4 8.6 %all-to-all-start = ((bf16[64,8,80]{2,1,0:T(8,128)(2,1)}), bf16[64,8,80]{2,1,0:T(8,128)(2,1)S(1)}, u32[]{:S(2)}, u32[]{:S(2)}) async-start(bf16[64,8,80]{2,1,0:T(8,128)(2,1)} %bitcast), calls=%async_computation | async-start | bytes 262144 | tf_op jit(solution)/shard_map/all_to_all | solution.py:49
  199.0 0.1 copy.20
  199.1 0.8 dynamic-slice
  200.0 15.2 %all-to-all-done = bf16[64,8,80]{2,1,0:T(8,128)(2,1)S(1)} async-done(((bf16[64,8,80]{2,1,0:T(8,128)(2,1)}), bf16[64,8,80]{2,1,0:T(8,128)(2,1)S(1)}, u32[]{:S(2)}, u32[]{:S(2)}) %all-to-all-start) | async-done | bytes 81952 | tf_op jit(solution)/shard_map/all_to_all | solution.py:49
  215.2 0.2 reshape.47
  215.4 0.2 multiply_reduce_fusion
  215.6 0.3 convolution_convert_fusion.1
  216.0 20.6 %all_to_all.23 = bf16[64,2,640]{2,1,0:T(2,128)(2,1)S(1)} all-to-all(bf16[64,2,640]{2,1,0:T(2,128)(2,1)S(1)} %reshape.43), channel_id=1, replica_groups=mesh['head'=8,'expert'=64] {'expert'}, dimensions={0} | all-to-all | bytes 327680 | tf_op jit(solution)/shard_map/all_to_all | solution.py:78
  236.6 0.7 reshape.44
  237.4 24.3 %all-gather.5.cloned.1.call-done = bf16[128,5120]{1,0:T(8,128)(2,1)} async-done(((bf16[128,640]{1,0:T(8,128)(2,1)}), bf16[128,5120]{1,0:T(8,128)(2,1)}) %all-gather.5.cloned.1.call-update) | async-done | bytes 1310736 | tf_op jit(solution)/shard_map/all_gather | solution.py:80
  261.6 2.0 fusion.1
  263.6 1.7 convolution_convert_fusion
  265.4 1.5 copy.22
  266.9 40.3 %reduce-scatter.4.cloned.1.call-done = bf16[640,128]{1,0:T(8,128)(2,1)} async-done(((bf16[5120,128]{1,0:T(8,128)(2,1)}), bf16[640,128]{1,0:T(8,128)(2,1)}) %reduce-scatter.4.cloned.1.call-update) | async-done | bytes 163856
  307.2 1.1 copy.23
  308.2 0.7 reshape.45
  309.0 14.4 %all-to-all-start.2 = ((bf16[64,2,640]{2,1,0:T(2,128)(2,1)}), bf16[64,2,640]{2,1,0:T(2,128)(2,1)S(1)}, u32[]{:S(2)}, u32[]{:S(2)}) async-start(bf16[64,2,640]{2,1,0:T(2,128)(2,1)} %reshape.45), calls=%async_computation.2 | async-start | bytes 327680 | tf_op jit(solution)/shard_map/all_to_all | solution.py:88
  323.4 0.1 copy.21
  323.5 0.1 select_reduce_fusion
  323.6 18.6 %all-to-all-done.2 = bf16[64,2,640]{2,1,0:T(2,128)(2,1)S(1)} async-done(((bf16[64,2,640]{2,1,0:T(2,128)(2,1)}), bf16[64,2,640]{2,1,0:T(2,128)(2,1)S(1)}, u32[]{:S(2)}, u32[]{:S(2)}) %all-to-all-start.2) | async-done | bytes 163872 | tf_op jit(solution)/shard_map/all_to_all | solution.py:88
  342.2 0.8 convolution_add_fusion.1
  (26 shorter events, 0.7 us)
Async XLA Ops:
  6.5 255.1 %copy-start = (bf16[1,2,96,5120]{3,2,1,0:T(8,128)(2,1)S(1)}, bf16[1,2,96,5120]{3,2,1,0:T(8,128)(2,1)}, u32[]{:S(2)}) copy-start(bf16[1,2,96,5120]{3,2,1,0:T(8,128)(2,1)} %param.22) | copy-start | bytes 5898244
  6.5 5.3 %copy-start.3 = (s32[8,6]{1,0:T(8,128)S(1)}, s32[8,6]{1,0:T(8,128)}, u32[]{:S(2)}) copy-start(s32[8,6]{1,0:T(8,128)} %param.20) | copy-start | bytes 580
  6.5 148.3 %copy-start.1 = (bf16[4096,80]{0,1:T(8,128)(2,1)S(1)}, bf16[4096,80]{0,1:T(8,128)(2,1)}, u32[]{:S(2)}) copy-start(bf16[4096,80]{0,1:T(8,128)(2,1)} %param.17) | copy-start | bytes 1966084
  6.5 148.3 %all-gather.3.cloned.1.call-start = ((), (), s32[]{:S(2)}) async-start(), calls=%async_computation.4 | async-start | bytes 4259840 | tf_op jit(solution)/shard_map/all_gather | solution.py:44
  158.4 57.0 %copy-start.2 = (bf16[8,5120]{1,0:T(8,128)(2,1)S(1)}, bf16[8,5120]{1,0:T(8,128)(2,1)}, u32[]{:S(2)}) copy-start(bf16[8,5120]{1,0:T(8,128)(2,1)} %param.18) | copy-start | bytes 245764
  190.4 24.8 %all-to-all-start = ((bf16[64,8,80]{2,1,0:T(8,128)(2,1)}), bf16[64,8,80]{2,1,0:T(8,128)(2,1)S(1)}, u32[]{:S(2)}, u32[]{:S(2)}) async-start(bf16[64,8,80]{2,1,0:T(8,128)(2,1)} %bitcast), calls=%async_computation | async-start | bytes 262144 | tf_op jit(solution)/shard_map/all_to_all | solution.py:49
  199.0 62.6 %all-gather.5.cloned.1.call-start = ((), (), s32[]{:S(2)}) async-start(), calls=%async_computation.5 | async-start | bytes 1474560 | tf_op jit(solution)/shard_map/all_gather | solution.py:80
  237.3 69.9 %reduce-scatter.4.cloned.1.call-start = ((), (), s32[]{:S(2)}) async-start(), calls=%async_computation.6 | async-start | bytes 1474560
  265.4 58.0 %copy-start.4 = (f32[8,6]{1,0:T(8,128)S(1)}, f32[8,6]{1,0:T(8,128)}, u32[]{:S(2)}) copy-start(f32[8,6]{1,0:T(8,128)} %param.21) | copy-start | bytes 580
  309.0 33.2 %all-to-all-start.2 = ((bf16[64,2,640]{2,1,0:T(2,128)(2,1)}), bf16[64,2,640]{2,1,0:T(2,128)(2,1)S(1)}, u32[]{:S(2)}, u32[]{:S(2)}) async-start(bf16[64,2,640]{2,1,0:T(2,128)(2,1)} %reshape.45), calls=%async_computation.2 | async-start | bytes 327680 | tf_op jit(solution)/shard_map/all_to_all | solution.py:88
Sparse Core Ops, SparseCore 0:
  11.9 142.8 all-gather.2
  237.4 24.1 all-gather.4
  267.0 40.1 reduce-scatter.3
where the time goes:
time: 350 us
  waiting for transfers between devices  241 us (69%)
  blocking collectives  51.8 us (15%)
  starting transfers between devices  23.1 us (7%)
  between operations  13.2 us (4%)
  matrix products  12.8 us (4%)
  local copies, waits for them, and re-layouts  6.85 us (2%)
    all_gather x1, waiting for transfers between devices, on_device(): lax.all_gather(flattened, 'expert', axis=0, tiled=True)  143 us
    unnamed x4, waiting for transfers between devices  40.4 us
    psum x1, blocking collectives, on_device(): column_sums = lax.psum(column_terms, 'head')  31.2 us
    all_gather x1, waiting for transfers between devices, on_device(): flat_rows = lax.all_gather(arrived_cols, 'head', axis=1, tiled=True)  24.3 us
    all_to_all x1, blocking collectives, on_device(): lax.all_to_all(outgoing, 'expert', split_axis=0, concat_axis=0, tiled=True)  20.6 us
    all_to_all x1, waiting for transfers between devices, on_device(): lax.all_to_all(summed_rows, 'expert', split_axis=0, concat_axis=0, tiled=...  18.6 us
    all_to_all x1, waiting for transfers between devices, on_device(): lax.all_to_all(column_sums.astype(jnp.bfloat16), 'expert', split_axis=0,...  15.2 us
    all_to_all x1, starting transfers between devices, on_device(): lax.all_to_all(summed_rows, 'expert', split_axis=0, concat_axis=0, tiled=...  14.4 us
  transfers between devices with their start and end apart: 5, of which 5 were waited for; matrix products, arithmetic and copies ran while one was open for 0% of the time, Pallas kernels for 0%

commit v1 on v0

--- a/solution.py
+++ b/solution.py
@@ -45,7 +45,7 @@
         w_value_out,
         preferred_element_type=jnp.float32,
     )
-    column_sums = lax.psum(column_terms, "head")
+    column_sums = jnp.sum(lax.all_gather(column_terms, "head"), axis=0)
     attention = lax.all_to_all(
         column_sums.astype(jnp.bfloat16), "expert", split_axis=0, concat_axis=1, tiled=True
     )

time: 350 us -> 361 us (1.031)
  waiting for transfers between devices: 241 us -> 274 us
  blocking collectives: 51.8 us -> 21.3 us
  starting transfers between devices: 23.1 us -> 29.7 us
    all_gather x0 -> x1, waiting for transfers between devices: none -> 32.9 us  [on_device(): column_sums = jnp.sum(lax.all_gather(column_terms, 'head'), axis=0)]
    psum x1 -> x0, blocking collectives: 31.2 us -> none  [on_device(): column_sums = lax.psum(column_terms, 'head')]
    all_to_all x1, starting transfers between devices: 8.61 us -> 15.2 us  [on_device(): lax.all_to_all(column_sums.astype(jnp.bfloat16), 'expert', split_axis=0,...]
    unnamed x4 -> x5, waiting for transfers between devices: 40.4 us -> 40.4 us
  transfers between devices with their start and end apart: 5 -> 6, of which waited for: 5 -> 6; matrix products, arithmetic and copies ran while one was open for 0% -> 0% of each run, Pallas kernels for 0% -> 0%
where the time goes in v1:
time: 361 us
  waiting for transfers between devices  274 us (76%)
  starting transfers between devices  29.7 us (8%)
  blocking collectives  21.3 us (6%)
  between operations  13.3 us (4%)
  matrix products  12.4 us (3%)
  local copies, waits for them, and re-layouts  9 us (2%)
    all_gather x1, waiting for transfers between devices, on_device(): lax.all_gather(flattened, 'expert', axis=0, tiled=True)  143 us
    unnamed x5, waiting for transfers between devices  40.4 us
    all_gather x1, waiting for transfers between devices, on_device(): column_sums = jnp.sum(lax.all_gather(column_terms, 'head'), axis=0)  32.9 us
    all_gather x1, waiting for transfers between devices, on_device(): flat_rows = lax.all_gather(arrived_cols, 'head', axis=1, tiled=True)  24.7 us
    all_to_all x1, blocking collectives, on_device(): lax.all_to_all(outgoing, 'expert', split_axis=0, concat_axis=0, tiled=True)  21.3 us
    all_to_all x1, waiting for transfers between devices, on_device(): lax.all_to_all(summed_rows, 'expert', split_axis=0, concat_axis=0, tiled=...  18.5 us
    all_to_all x1, starting transfers between devices, on_device(): lax.all_to_all(column_sums.astype(jnp.bfloat16), 'expert', split_axis=0,...  15.2 us
    all_to_all x1, waiting for transfers between devices, on_device(): lax.all_to_all(column_sums.astype(jnp.bfloat16), 'expert', split_axis=0,...  14.5 us
  transfers between devices with their start and end apart: 6, of which 6 were waited for; matrix products, arithmetic and copies ran while one was open for 0% of the time, Pallas kernels for 0%

profile of v1, /device:TPU:7, one launch (start us, length us, event | category | flops | bytes accessed | tf_op | source)
XLA Modules:
  0.0 360.8 jit_solution(6892368965744753505)
XLA Ops:
  6.5 1.8 fusion.21
  8.3 1.1 fusion.8
  9.4 0.2 fusion.20
  9.6 0.3 fusion.4
  9.9 0.7 copy.22
  10.6 143.0 %all-gather.5.cloned.1.call-done = bf16[512,4096]{1,0:T(8,128)(2,1)} async-done(((bf16[8,4096]{1,0:T(8,128)(2,1)}), bf16[512,4096]{1,0:T(8,128)(2,1)}) %all-gather.5.cloned.1.call-update) | async-done | bytes 4194320 | tf_op jit(solution)/shard_map/all_gather | solution.py:44
  153.6 4.4 %fusion.22 = f32[512,80]{0,1:T(8,128)} fusion(bf16[512,4096]{1,0:T(8,128)(2,1)} %all-gather.5.cloned.1.call-done, bf16[4096,80]{0,1:T(8,128)(2,1)} %param.17), kind=kOutput, calls=%fused_computation.41 | convolution fusion | flops 335544320 | bytes 5013504 | tf_op jit(solution)/shard_map/dot_general | solution.py:43
  158.3 0.2 select_reduce_fusion.1
  158.6 32.9 %all-gather.9.cloned.1.call-done = f32[4096,80]{0,1:T(8,128)} async-done(((f32[512,80]{0,1:T(8,128)}), f32[4096,80]{0,1:T(8,128)}) %all-gather.9.cloned.1.call-update) | async-done | bytes 1310736 | tf_op jit(solution)/shard_map/all_gather | solution.py:48
  191.5 2.1 copy.23
  193.6 0.3 bitcast_reduce_fusion
  194.0 0.7 copy.16
  194.7 15.2 %all-to-all-start = ((bf16[64,8,80]{2,1,0:T(8,128)(2,1)}), bf16[64,8,80]{2,1,0:T(8,128)(2,1)S(1)}, u32[]{:S(2)}, u32[]{:S(2)}) async-start(bf16[64,8,80]{2,1,0:T(8,128)(2,1)} %bitcast), calls=%async_computation | async-start | bytes 262144 | tf_op jit(solution)/shard_map/all_to_all | solution.py:49
  209.9 0.1 copy.18
  210.0 0.8 dynamic-slice
  210.8 14.5 %all-to-all-done = bf16[64,8,80]{2,1,0:T(8,128)(2,1)S(1)} async-done(((bf16[64,8,80]{2,1,0:T(8,128)(2,1)}), bf16[64,8,80]{2,1,0:T(8,128)(2,1)S(1)}, u32[]{:S(2)}, u32[]{:S(2)}) %all-to-all-start) | async-done | bytes 81952 | tf_op jit(solution)/shard_map/all_to_all | solution.py:49
  225.4 0.2 reshape.49
  225.6 0.2 multiply_reduce_fusion
  225.7 0.3 convolution_convert_fusion.1
  226.1 21.3 %all_to_all.20 = bf16[64,2,640]{2,1,0:T(2,128)(2,1)S(1)} all-to-all(bf16[64,2,640]{2,1,0:T(2,128)(2,1)S(1)} %reshape.45), channel_id=1, replica_groups=mesh['head'=8,'expert'=64] {'expert'}, dimensions={0} | all-to-all | bytes 327680 | tf_op jit(solution)/shard_map/all_to_all | solution.py:78
  247.5 0.7 reshape.46
  248.3 24.7 %all-gather.7.cloned.1.call-done = bf16[128,5120]{1,0:T(8,128)(2,1)} async-done(((bf16[128,640]{1,0:T(8,128)(2,1)}), bf16[128,5120]{1,0:T(8,128)(2,1)}) %all-gather.7.cloned.1.call-update) | async-done | bytes 1310736 | tf_op jit(solution)/shard_map/all_gather | solution.py:80
  273.0 2.0 fusion.1
  275.0 1.7 convolution_convert_fusion
  276.7 1.5 copy.20
  278.2 40.3 %reduce-scatter.4.cloned.1.call-done = bf16[640,128]{1,0:T(8,128)(2,1)} async-done(((bf16[5120,128]{1,0:T(8,128)(2,1)}), bf16[640,128]{1,0:T(8,128)(2,1)}) %reduce-scatter.4.cloned.1.call-update) | async-done | bytes 163856
  318.5 1.1 copy.21
  319.6 0.7 reshape.47
  320.3 14.4 %all-to-all-start.2 = ((bf16[64,2,640]{2,1,0:T(2,128)(2,1)}), bf16[64,2,640]{2,1,0:T(2,128)(2,1)S(1)}, u32[]{:S(2)}, u32[]{:S(2)}) async-start(bf16[64,2,640]{2,1,0:T(2,128)(2,1)} %reshape.47), calls=%async_computation.2 | async-start | bytes 327680 | tf_op jit(solution)/shard_map/all_to_all | solution.py:88
  334.8 0.1 copy.19
  334.9 18.5 %all-to-all-done.2 = bf16[64,2,640]{2,1,0:T(2,128)(2,1)S(1)} async-done(((bf16[64,2,640]{2,1,0:T(2,128)(2,1)}), bf16[64,2,640]{2,1,0:T(2,128)(2,1)S(1)}, u32[]{:S(2)}, u32[]{:S(2)}) %all-to-all-start.2) | async-done | bytes 163872 | tf_op jit(solution)/shard_map/all_to_all | solution.py:88
  353.5 0.8 convolution_add_fusion.1
  (30 shorter events, 0.9 us)
Async XLA Ops:
  6.5 266.5 %copy-start = (bf16[1,2,96,5120]{3,2,1,0:T(8,128)(2,1)S(1)}, bf16[1,2,96,5120]{3,2,1,0:T(8,128)(2,1)}, u32[]{:S(2)}) copy-start(bf16[1,2,96,5120]{3,2,1,0:T(8,128)(2,1)} %param.22) | copy-start | bytes 5898244
  6.5 3.0 copy-start.1
  6.5 147.1 %all-gather.5.cloned.1.call-start = ((), (), s32[]{:S(2)}) async-start(), calls=%async_computation.4 | async-start | bytes 4259840 | tf_op jit(solution)/shard_map/all_gather | solution.py:44
  10.6 147.5 %copy-start.3 = (s32[8,6]{1,0:T(8,128)S(1)}, s32[8,6]{1,0:T(8,128)}, u32[]{:S(2)}) copy-start(s32[8,6]{1,0:T(8,128)} %param.20) | copy-start | bytes 580
  10.6 180.9 %all-gather.9.cloned.1.call-start = ((), (), s32[]{:S(2)}) async-start(), calls=%async_computation.6 | async-start | bytes 1474560 | tf_op jit(solution)/shard_map/all_gather | solution.py:48
  193.6 32.0 %copy-start.2 = (bf16[8,5120]{1,0:T(8,128)(2,1)S(1)}, bf16[8,5120]{1,0:T(8,128)(2,1)}, u32[]{:S(2)}) copy-start(bf16[8,5120]{1,0:T(8,128)(2,1)} %param.18) | copy-start | bytes 245764
  194.7 30.6 %all-to-all-start = ((bf16[64,8,80]{2,1,0:T(8,128)(2,1)}), bf16[64,8,80]{2,1,0:T(8,128)(2,1)S(1)}, u32[]{:S(2)}, u32[]{:S(2)}) async-start(bf16[64,8,80]{2,1,0:T(8,128)(2,1)} %bitcast), calls=%async_computation | async-start | bytes 262144 | tf_op jit(solution)/shard_map/all_to_all | solution.py:49
  209.9 63.1 %all-gather.7.cloned.1.call-start = ((), (), s32[]{:S(2)}) async-start(), calls=%async_computation.5 | async-start | bytes 1474560 | tf_op jit(solution)/shard_map/all_gather | solution.py:80
  248.2 70.3 %reduce-scatter.4.cloned.1.call-start = ((), (), s32[]{:S(2)}) async-start(), calls=%async_computation.7 | async-start | bytes 1474560
  278.2 56.6 %copy-start.4 = (f32[8,6]{1,0:T(8,128)S(1)}, f32[8,6]{1,0:T(8,128)}, u32[]{:S(2)}) copy-start(f32[8,6]{1,0:T(8,128)} %param.21) | copy-start | bytes 580
  320.3 33.1 %all-to-all-start.2 = ((bf16[64,2,640]{2,1,0:T(2,128)(2,1)}), bf16[64,2,640]{2,1,0:T(2,128)(2,1)S(1)}, u32[]{:S(2)}, u32[]{:S(2)}) async-start(bf16[64,2,640]{2,1,0:T(2,128)(2,1)} %reshape.47), calls=%async_computation.2 | async-start | bytes 327680 | tf_op jit(solution)/shard_map/all_to_all | solution.py:88
Sparse Core Ops, SparseCore 0:
  10.7 142.8 all-gather.4
  158.2 33.2 all-gather.8
  248.3 24.6 all-gather.6
  278.3 40.1 reduce-scatter.3
